TPU v7x, 256 devices: a whole 4x4x8 slice. The times are simulated.
256 devices in a mesh: dp: 64 (over z, y, core), mp: 4 (over x).
Axes of the slice: x: 4, y: 4, z: 8, core: 2. Of those that a mesh axis runs over, the one named last changes fastest.
Arguments:
- tree_query: bfloat16 [8192, 2048], P('dp', 'mp'), may hold values from -6 to 6
- new_kv: bfloat16 [8192, 2, 512], P('dp', None, 'mp'), may hold values from -6 to 6
- kv_cache: bfloat16 [2560, 2, 128, 512], P('dp', None, None, 'mp'), may hold values from -4 to 4
- page_table: int32 [128, 32], P('dp'), may hold values from 0 to 39, as said below
- cache_len: int32 [128], P('dp'), may hold values from 2 to 4096, as said below
- tree_mask: int32 [128, 64, 64], P('dp'), may hold values from 0 to 1, as said below
- out_weight: bfloat16 [2048, 2048], P('mp'), may hold values from -0.5 to 0.5
- residual_in: bfloat16 [8192, 2048], P('dp'), may hold values from -3 to 3
- norm_gain: float32 [2048], replicated, may hold values from 0.25 to 1.75
- route_ids: int32 [8192, 6], P('dp'), may hold values from 0 to 63, all different within a row; in each aligned block of 128 rows (0 to 127, 128 to 255, ...) at most 16 rows name the same one
- route_weight: float32 [8192, 6], P('dp'), may hold values from 0.05 to 0.5
- w_gate: bfloat16 [64, 2048, 1408], P('dp', None, 'mp'), may hold values from -0.125 to 0.125
- w_up: bfloat16 [64, 2048, 1408], P('dp', None, 'mp'), may hold values from -0.125 to 0.125
- w_down: bfloat16 [64, 1408, 2048], P('dp', None, 'mp'), may hold values from -0.15625 to 0.15625
- shared_gate: bfloat16 [2048, 2816], P('dp', 'mp'), may hold values from -0.125 to 0.125
- shared_up: bfloat16 [2048, 2816], P('dp', 'mp'), may hold values from -0.125 to 0.125
- shared_down: bfloat16 [2816, 2048], P('mp', 'dp'), may hold values from -0.109375 to 0.109375
Outputs:
- layer_out: bfloat16 [8192, 2048], P('dp', 'mp')
Inputs may be any that keep to these rules, and one draw needn't show every extreme that they name: `route_ids`: each row names 6 different experts. Within the rows of one index of dp (aligned blocks of 128 rows) no expert is named by more than 16 rows, and in some block one expert is named by exactly 16 rows. `cache_len`: the pages of the requests of one index of dp number at most 40 together; some request has exactly 4096 cached positions. `page_table`: entry [r, j] is the slot, in the pool of the index of dp that holds request r, of the page with cache positions j * 128 to j * 128 + 127. Entries with j * 128 < cache_len[r] are distinct over the requests of one index of dp; the other entries are valid slots whose contents are not read. tree_mask[r, i, u] is 1 where tree node u is node i or an ancestor of it, else 0; node 0 is the root and each other node's parent has a smaller index.
All inputs are finite; a program needn't handle non-finite values.
Results may differ from a plain program's by a relative error of at most 0.009.
Values may be sent and summed in bfloat16 or wider, within the bound.
No kernel may reach another device: no remote copies, remote signals or barrier semaphores. Data moves between devices by JAX's collectives and lax.ppermute only.
A program may use at most 128 MiB of HBM per device.

v0:
```python
import jax
import jax.numpy as jnp
from jax import lax
from jax.sharding import PartitionSpec as P

NEGATIVE_FILL = -1e30
EPSILON = 1e-05


def normalize(rows, gain):
    values = rows.astype(jnp.float32)
    mean_square = jnp.mean(values * values, axis=-1, keepdims=True)
    return (values * lax.rsqrt(mean_square + EPSILON) * gain).astype(jnp.bfloat16)


def attend_requests(
    queries, tree_keys, tree_values, tree_allow, kv_cache, page_table, cache_len, score_scale
):

    def per_request(request_item):
        q_rows, own_keys, own_values, allow_rows, table_row, length = request_item
        kv_pages = kv_cache[table_row]
        cache_keys = kv_pages[:, 0].reshape(-1, kv_pages.shape[-1])
        cache_values = kv_pages[:, 1].reshape(-1, kv_pages.shape[-1])
        live_mask = (jnp.arange(cache_keys.shape[0], dtype=jnp.int32) < length)[None, :]
        cache_scores = (
            jnp.einsum("qd,kd->qk", q_rows, cache_keys, preferred_element_type=jnp.float32)
            * score_scale
        )
        cache_scores = jnp.where(live_mask, cache_scores, NEGATIVE_FILL)
        tree_scores = (
            jnp.einsum("qd,ud->qu", q_rows, own_keys, preferred_element_type=jnp.float32)
            * score_scale
        )
        tree_scores = jnp.where(allow_rows, tree_scores, NEGATIVE_FILL)
        row_peak = jnp.maximum(jnp.max(cache_scores, axis=1), jnp.max(tree_scores, axis=1))[:, None]
        cache_probs = jnp.where(live_mask, jnp.exp(cache_scores - row_peak), 0.0)
        tree_probs = jnp.where(allow_rows, jnp.exp(tree_scores - row_peak), 0.0)
        denom_sum = jnp.sum(cache_probs, axis=1) + jnp.sum(tree_probs, axis=1)
        weighted = jnp.dot(
            cache_probs.astype(jnp.bfloat16), cache_values, preferred_element_type=jnp.float32
        )
        weighted = weighted + jnp.dot(
            tree_probs.astype(jnp.bfloat16), own_values, preferred_element_type=jnp.float32
        )
        return (weighted / denom_sum[:, None]).astype(jnp.bfloat16)

    return lax.map(
        per_request, (queries, tree_keys, tree_values, tree_allow, page_table, cache_len)
    )


def run_experts(rows, w_gate, w_up, w_down):
    source_count, slot_count, model_width = rows.shape
    flat_rows = rows.reshape(source_count * slot_count, model_width)
    gate_proj = jnp.dot(flat_rows, w_gate[0], preferred_element_type=jnp.float32)
    up_proj = jnp.dot(flat_rows, w_up[0], preferred_element_type=jnp.float32)
    hidden_act = (jax.nn.silu(gate_proj) * up_proj).astype(jnp.bfloat16)
    down_rows = w_down[0]
    summed = jnp.dot(
        lax.all_gather(hidden_act, "mp", axis=1, tiled=True),
        down_rows,
        preferred_element_type=jnp.float32,
    )
    outputs = summed.astype(jnp.bfloat16).reshape(source_count, slot_count, w_down.shape[2])
    return lax.all_to_all(outputs, "dp", split_axis=0, concat_axis=0, tiled=True)


def shared_experts(normed_rows, shared_gate, shared_up, shared_down):
    gate_total = jnp.dot(
        normed_rows,
        lax.all_gather(shared_gate, "dp", axis=0, tiled=True),
        preferred_element_type=jnp.float32,
    )
    up_total = jnp.dot(
        normed_rows,
        lax.all_gather(shared_up, "dp", axis=0, tiled=True),
        preferred_element_type=jnp.float32,
    )
    shared_hidden = (jax.nn.silu(gate_total) * up_total).astype(jnp.bfloat16)
    terms = jnp.dot(
        shared_hidden,
        lax.all_gather(shared_down, "dp", axis=1, tiled=True),
        preferred_element_type=jnp.float32,
    )
    return lax.psum_scatter(terms.astype(jnp.bfloat16), "mp", scatter_dimension=1, tiled=True)


def on_device(
    tree_query,
    new_kv,
    kv_cache,
    page_table,
    cache_len,
    tree_mask,
    out_weight,
    residual_in,
    norm_gain,
    route_ids,
    route_weight,
    w_gate,
    w_up,
    w_down,
    shared_gate,
    shared_up,
    shared_down,
):
    tok_rows = tree_query.shape[0]
    req_count = cache_len.shape[0]
    tree_len = tree_mask.shape[1]
    head_width = new_kv.shape[2]
    local_heads = tree_query.shape[1] // head_width
    score_scale = head_width ** (-0.5)
    queries = tree_query.reshape(req_count, tree_len, local_heads, head_width)
    queries = queries.transpose(0, 2, 1, 3).reshape(req_count, local_heads * tree_len, head_width)
    tree_keys = new_kv[:, 0, :].reshape(req_count, tree_len, head_width)
    tree_values = new_kv[:, 1, :].reshape(req_count, tree_len, head_width)
    tree_allow = jnp.tile(tree_mask, (1, local_heads, 1)) == 1
    attended = attend_requests(
        queries, tree_keys, tree_values, tree_allow, kv_cache, page_table, cache_len, score_scale
    )
    attended = attended.reshape(req_count, local_heads, tree_len, head_width).transpose(0, 2, 1, 3)
    attended = attended.reshape(tok_rows, local_heads * head_width)
    partial_value = jnp.dot(attended, out_weight, preferred_element_type=jnp.float32)
    model_width = residual_in.shape[1]
    quarter = model_width // lax.axis_size("mp")
    col_start = lax.axis_index("mp") * quarter
    experts = lax.axis_size("dp") * w_gate.shape[0]
    route_count = route_ids.shape[1]
    capacity = min(tok_rows, 4 * tok_rows * route_count // (3 * experts))
    expert_ids = route_ids.reshape(-1)
    onehot = (expert_ids[:, None] == jnp.arange(experts, dtype=jnp.int32)[None, :]).astype(
        jnp.int32
    )
    slot_index = jnp.sum((jnp.cumsum(onehot, axis=0) - onehot) * onehot, axis=1)
    sources = jnp.arange(expert_ids.shape[0], dtype=jnp.int32) // route_count
    summed_heads = lax.psum(partial_value, "mp")
    stream = (residual_in.astype(jnp.float32) + summed_heads).astype(jnp.bfloat16)
    own_stream = lax.dynamic_slice_in_dim(stream, col_start, quarter, 1)
    normed_rows = normalize(stream, norm_gain)
    buffer = jnp.zeros((experts, capacity, normed_rows.shape[1]), jnp.bfloat16)
    results = run_experts(
        lax.all_to_all(
            buffer.at[expert_ids, slot_index].set(normed_rows[sources]),
            "dp",
            split_axis=0,
            concat_axis=0,
            tiled=True,
        ),
        w_gate,
        w_up,
        w_down,
    )
    shared_out = shared_experts(normed_rows, shared_gate, shared_up, shared_down)
    result_rows = results.reshape(experts * capacity, quarter)
    picked = (
        result_rows[expert_ids * capacity + slot_index]
        .reshape(tok_rows, route_count, quarter)
        .astype(jnp.float32)
    )
    mixture = jnp.einsum("tk,tkc->tc", route_weight, picked, precision=lax.Precision.HIGHEST)
    return (own_stream.astype(jnp.float32) + shared_out.astype(jnp.float32) + mixture).astype(
        jnp.bfloat16
    )


def solution(mesh):
    return jax.shard_map(
        on_device,
        mesh=mesh,
        in_specs=(
            P("dp", "mp"),
            P("dp", None, "mp"),
            P("dp", None, None, "mp"),
            P("dp", None),
            P("dp"),
            P("dp", None, None),
            P("mp", None),
            P("dp", None),
            P(),
            P("dp", None),
            P("dp", None),
            P("dp", None, "mp"),
            P("dp", None, "mp"),
            P("dp", None, "mp"),
            P("dp", "mp"),
            P("dp", "mp"),
            P("mp", "dp"),
        ),
        out_specs=P("dp", "mp"),
        check_vma=False,
    )
```

profile of v0, /device:TPU:8, one launch (start us, length us, event | category | flops | bytes accessed | tf_op | source)
XLA Modules:
  0.0 659.3 jit_solution(10278691214841616985)
XLA Ops:
  9.9 21.6 %while.10 = (s32[]{:T(128)}, bf16[2,256,128]{2,1,0:T(8,128)(2,1)S(1)}, s32[2]{0:T(128)}, bf16[2,256,128]{2,1,0:T(8,128)(2,1)S(1)}, s32[2,32]{1,0:T(2,128)}, /*in...) while((s32[]{:T(128)}, ...), condition=%wide.region_5.6_spmd, body=%wide.region_0.5_spmd.sunk | while | flops 554947200 | bytes 23845564 | solution.py:48
  10.6 3.9 gather_fusion
  14.5 1.7 fusion.101
  21.4 3.9 gather_fusion
  25.3 1.7 fusion.101
  33.8 1.8 reduce-window.6
  36.1 51.0 %all-reduce.2.cloned.1.call-done = f32[128,2048]{1,0:T(8,128)} async-done(((f32[128,2048]{1,0:T(8,128)}), f32[128,2048]{1,0:T(8,128)}) %all-reduce.2.cloned.1.call-update) | async-done | bytes 1048592 | tf_op jit(solution)/shard_map/psum | solution.py:137
  89.6 4.3 gather_fusion.1
  93.9 2.4 broadcast_in_dim.47
  96.3 137.9 %scatter_fusion = bf16[64,16,2048]{2,1,0:T(8,128)(2,1)} fusion(bf16[64,16,2048]{2,1,0:T(8,128)(2,1)} %broadcast_in_dim.47, s32[768]{0:T(1024)S(1)} %get-tuple-element.54, bf16[768,2048]{1,0:T(8,128)(2,1)} %gather_fusion.1), kind=kCustom, calls=%fused_computation.3 | custom fusion | bytes 9443328 | tf_op jit(solution)/shard_map/scatter | solution.py:144
  234.3 106.9 %all_to_all.10 = bf16[64,16,2048]{2,1,0:T(8,128)(2,1)S(1)} all-to-all(bf16[64,16,2048]{2,1,0:T(8,128)(2,1)} %scatter_fusion), channel_id=1, replica_groups=mesh['dp'=64,'mp'=4] {'dp'}, dimensions={0} | all-to-all | bytes 8388608 | tf_op jit(solution)/shard_map/all_to_all | solution.py:143
  341.2 1.8 fusion.35
  343.0 2.7 fusion.37
  347.6 33.9 %all-gather.11.cloned.1.call-done = bf16[1024,1408]{0,1:T(8,128)(2,1)} async-done(((bf16[1024,352]{0,1:T(8,128)(2,1)}), bf16[1024,1408]{0,1:T(8,128)(2,1)}) %all-gather.11.cloned.1.call-update) | async-done | bytes 2883600 | tf_op jit(solution)/shard_map/all_gather | solution.py:61
  381.5 5.1 convolution_convert_fusion.1
  386.6 10.7 %all-to-all-start.1 = ((bf16[64,16,512]{2,1,0:T(8,128)(2,1)}), bf16[64,16,512]{2,1,0:T(8,128)(2,1)}, u32[]{:S(2)}, u32[]{:S(2)}) async-start(bf16[64,16,512]{2,1,0:T(8,128)(2,1)} %bitcast.139), calls=%async_computation.2 | async-start | bytes 2097152 | tf_op jit(solution)/shard_map/all_to_all | solution.py:66
  397.4 66.0 %all-gather.5.cloned.1.call-done = bf16[2048,704]{1,0:T(8,128)(2,1)} async-done(((bf16[32,704]{1,0:T(8,128)(2,1)}), bf16[2048,704]{1,0:T(8,128)(2,1)}) %all-gather.5.cloned.1.call-update) | async-done | bytes 2883600 | tf_op jit(solution)/shard_map/all_gather | solution.py:72
  463.4 3.2 fusion.67
  466.6 75.6 %all-gather.7.cloned.1.call-done = bf16[2048,704]{1,0:T(8,128)(2,1)} async-done(((bf16[32,704]{1,0:T(8,128)(2,1)}), bf16[2048,704]{1,0:T(8,128)(2,1)}) %all-gather.7.cloned.1.call-update) | async-done | bytes 2883600 | tf_op jit(solution)/shard_map/all_gather | solution.py:77
  542.2 78.8 %all-gather.9.cloned.1.call-done = bf16[704,2048]{0,1:T(8,128)(2,1)} async-done(((bf16[704,32]{0,1:T(8,128)(2,1)}), bf16[704,2048]{0,1:T(8,128)(2,1)}) %all-gather.9.cloned.1.call-update) | async-done | bytes 2883600 | tf_op jit(solution)/shard_map/all_gather | solution.py:83
  621.0 7.0 %convolution_convert_fusion = bf16[128,2048]{1,0:T(8,128)(2,1)} fusion(bf16[704,2048]{0,1:T(8,128)(2,1)} %all-gather.9.cloned.1.call-done, bf16[128,2048]{1,0:T(8,128)(2,1)S(1)} %fusion.43, bf16[2048,704]{1,0:T(8,128)(2,1)} %all-gather.7.cloned.1.call-done, f32[128,704]{0,1:T(8,128)S(1)} %fusion.67), kind=kOutput, calls=%fused_computation.44 | convolution fusion | flops 739000320 | bytes 7176192 | tf_op jit(solution)/shard_map/dot_general | solution.py:81
  628.2 4.7 gather_fusion.2
  635.2 15.5 %reduce-scatter.2.cloned.1.call-done = bf16[128,512]{1,0:T(8,128)(2,1)} async-done(((bf16[128,2048]{1,0:T(8,128)(2,1)}), bf16[128,512]{1,0:T(8,128)(2,1)}) %reduce-scatter.2.cloned.1.call-update) | async-done | bytes 131088 | tf_op jit(solution)/shard_map/reduce_scatter | solution.py:86
  650.8 1.7 fusion.49
  (87 shorter events, 23.1 us)
Async XLA Ops:
  6.5 25.1 %copy-start = (bf16[512,2048]{1,0:T(8,128)(2,1)S(1)}, bf16[512,2048]{1,0:T(8,128)(2,1)}, u32[]{:S(2)}) copy-start(bf16[512,2048]{1,0:T(8,128)(2,1)} %param.25) | copy-start | bytes 6291460
  6.5 80.6 %all-reduce.2.cloned.1.call-start = ((), (), s32[]{:S(2)}) async-start(), calls=%async_computation.3 | async-start | bytes 2097152 | tf_op jit(solution)/shard_map/psum | solution.py:137
  14.5 1.7 copy-start.8
  25.3 1.7 copy-start.8
  31.5 1.7 copy-start.4
  31.5 55.6 %copy-start.2 = (bf16[128,2048]{1,0:T(8,128)(2,1)S(1)}, bf16[128,2048]{1,0:T(8,128)(2,1)}, u32[]{:S(2)}) copy-start(bf16[128,2048]{1,0:T(8,128)(2,1)} %param.26) | copy-start | bytes 1572868
  31.6 57.8 %copy-start.3 = (f32[2048]{0:T(1024)S(1)}, f32[2048]{0:T(1024)}, u32[]{:S(2)}) copy-start(f32[2048]{0:T(1024)} %param.27) | copy-start | bytes 24580
  33.2 348.4 %all-gather.11.cloned.1.call-start = ((), (), s32[]{:S(2)}) async-start(), calls=%async_computation.8 | async-start | bytes 3604480 | tf_op jit(solution)/shard_map/all_gather | solution.py:61
  88.6 0.8 copy-start.1
  234.3 106.9 %copy-start.6 = (bf16[1,2048,352]{1,2,0:T(8,128)(2,1)S(1)}, bf16[1,2048,352]{1,2,0:T(8,128)(2,1)}, u32[]{:S(2)}) copy-start(bf16[1,2048,352]{1,2,0:T(8,128)(2,1)} %param.30) | copy-start | bytes 4325380
  341.2 1.8 copy-start.7
  345.7 117.7 %all-gather.5.cloned.1.call-start = ((), (), s32[]{:S(2)}) async-start(), calls=%async_computation.4 | async-start | bytes 3194880 | tf_op jit(solution)/shard_map/all_gather | solution.py:72
  346.4 195.8 %all-gather.7.cloned.1.call-start = ((), (), s32[]{:S(2)}) async-start(), calls=%async_computation.5 | async-start | bytes 3194880 | tf_op jit(solution)/shard_map/all_gather | solution.py:77
  347.0 274.0 %all-gather.9.cloned.1.call-start = ((), (), s32[]{:S(2)}) async-start(), calls=%async_computation.6 | async-start | bytes 3194880 | tf_op jit(solution)/shard_map/all_gather | solution.py:83
  386.6 241.6 %all-to-all-start.1 = ((bf16[64,16,512]{2,1,0:T(8,128)(2,1)}), bf16[64,16,512]{2,1,0:T(8,128)(2,1)}, u32[]{:S(2)}, u32[]{:S(2)}) async-start(bf16[64,16,512]{2,1,0:T(8,128)(2,1)} %bitcast.139), calls=%async_computation.2 | async-start | bytes 2097152 | tf_op jit(solution)/shard_map/all_to_all | solution.py:66
  397.4 253.4 %reduce-scatter.2.cloned.1.call-start = ((), (), s32[]{:S(2)}) async-start(), calls=%async_computation.7 | async-start | bytes 655360 | tf_op jit(solution)/shard_map/reduce_scatter | solution.py:86
  466.6 161.4 %copy-start.5 = (f32[128,6]{0,1:T(8,128)S(1)}, f32[128,6]{0,1:T(8,128)}, u32[]{:S(2)}) copy-start(f32[128,6]{0,1:T(8,128)} %param.29) | copy-start | bytes 9220
Sparse Core Ops, SparseCore 0:
  33.3 53.8 all-reduce.1
  345.8 35.6 all-gather.10
  384.7 78.7 all-gather.4
  466.4 75.7 all-gather.6
  545.2 75.7 all-gather.8
  628.2 22.5 reduce-scatter.1
where the time goes:
time: 663 us; the launch traced here: 659 us
  waiting for transfers between devices  323 us (49%)
  local copies, waits for them, and re-layouts  168 us (25%)
  blocking collectives  107 us (16%)
  matrix products  26.4 us (4%)
  between operations  13.7 us (2%)
  starting transfers between devices  10.9 us (2%)
  other arithmetic  10.9 us (2%)
    scatter x1, local copies, waits for them, and re-layouts, on_device(): buffer.at[expert_ids, slot_index].set(normed_rows[sources])  138 us
    all_to_all x1, blocking collectives, on_device(): lax.all_to_all(buffer.at[expert_ids, slot_index].set(normed_rows[sources]...  107 us
    all_gather x1, waiting for transfers between devices, shared_experts(): lax.all_gather(shared_down, 'dp', axis=1, tiled=True)  78.8 us
    all_gather x1, waiting for transfers between devices, shared_experts(): lax.all_gather(shared_up, 'dp', axis=0, tiled=True)  75.6 us
    all_gather x1, waiting for transfers between devices, shared_experts(): lax.all_gather(shared_gate, 'dp', axis=0, tiled=True)  66 us
    psum x1, waiting for transfers between devices, on_device(): summed_heads = lax.psum(partial_value, 'mp')  51 us
    all_gather x1, waiting for transfers between devices, run_experts(): lax.all_gather(hidden_act, 'mp', axis=1, tiled=True)  33.9 us
    reduce_scatter x1, waiting for transfers between devices, shared_experts(): lax.psum_scatter(terms.astype(jnp.bfloat16), 'mp', scatter_dimension=1, t...  15.5 us
  transfers between devices with their start and end apart: 7, of which 6 were waited for; matrix products, arithmetic and copies ran while one was open for 4% of the time, Pallas kernels for 0%

commit v1 on v0

--- a/solution.py
+++ b/solution.py
@@ -2,6 +2,7 @@
 import jax.numpy as jnp
 from jax import lax
 from jax.sharding import PartitionSpec as P
+from jax.lax import axis_index, axis_size, ppermute
 
 NEGATIVE_FILL = -1e30
 EPSILON = 1e-05
@@ -51,6 +52,28 @@
 
 
 def run_experts(rows, w_gate, w_up, w_down):
+
+    def carry_spans_over_axis(z, chip_axis):
+        met_up, current_value, kept_arr = (axis_size(chip_axis), axis_index(chip_axis), z.shape[1])
+        found = [j0 * met_up if b == 1 else j0 for b, j0 in enumerate(z.shape)]
+        block_now = lax.dynamic_update_slice_in_dim(
+            jnp.zeros(found, z.dtype), z, current_value * kept_arr, axis=1
+        )
+        n_now = view_out = z
+        for no in [*range(1, met_up // 2 + 1)]:
+            n_now = ppermute(n_now, chip_axis, [(b, (b + 1) % met_up) for b in range(met_up)])
+            block_now = lax.dynamic_update_slice_in_dim(
+                block_now, n_now, (current_value - no) % met_up * kept_arr, axis=1
+            )
+            if 2 * no < met_up:
+                view_out = ppermute(
+                    view_out, chip_axis, [(b, (b - 1) % met_up) for b in range(met_up)]
+                )
+                block_now = lax.dynamic_update_slice_in_dim(
+                    block_now, view_out, (current_value + no) % met_up * kept_arr, axis=1
+                )
+        return block_now
+
     source_count, slot_count, model_width = rows.shape
     flat_rows = rows.reshape(source_count * slot_count, model_width)
     gate_proj = jnp.dot(flat_rows, w_gate[0], preferred_element_type=jnp.float32)
@@ -58,9 +81,7 @@
     hidden_act = (jax.nn.silu(gate_proj) * up_proj).astype(jnp.bfloat16)
     down_rows = w_down[0]
     summed = jnp.dot(
-        lax.all_gather(hidden_act, "mp", axis=1, tiled=True),
-        down_rows,
-        preferred_element_type=jnp.float32,
+        carry_spans_over_axis(hidden_act, "mp"), down_rows, preferred_element_type=jnp.float32
     )
     outputs = summed.astype(jnp.bfloat16).reshape(source_count, slot_count, w_down.shape[2])
     return lax.all_to_all(outputs, "dp", split_axis=0, concat_axis=0, tiled=True)

time: 663 us -> 466 us (0.70)
  waiting for transfers between devices: 323 us -> 205 us
  blocking collectives: 107 us -> 0 us
  starting transfers between devices: 10.9 us -> 25.1 us
    all_to_all x1 -> x0, blocking collectives: 107 us -> none  [on_device(): lax.all_to_all(buffer.at[expert_ids, slot_index].set(normed_rows[sources]...]
    all_to_all x0 -> x1, waiting for transfers between devices: none -> 104 us  [on_device(): lax.all_to_all(buffer.at[expert_ids, slot_index].set(normed_rows[sources]...]
    all_gather x1, waiting for transfers between devices: 75.6 us -> 0.03 us  [shared_experts(): lax.all_gather(shared_up, 'dp', axis=0, tiled=True)]
    all_gather x1, waiting for transfers between devices: 78.8 us -> 5.13 us  [shared_experts(): lax.all_gather(shared_down, 'dp', axis=1, tiled=True)]
    all_gather x1, waiting for transfers between devices: 66 us -> 0.03 us  [shared_experts(): lax.all_gather(shared_gate, 'dp', axis=0, tiled=True)]
    all_gather x1 -> x0, waiting for transfers between devices: 33.9 us -> none  [run_experts(): lax.all_gather(hidden_act, 'mp', axis=1, tiled=True)]
    ppermute x0 -> x3, waiting for transfers between devices: none -> 27.7 us  [the longest x2 27.7 us: carry_spans_over_axis(): ppermute(n_now, chip_axis, [(b, (b + 1) % met_up) for b in range(met_up)])]
    all_to_all x1, waiting for transfers between devices: 0.01 us -> 12.9 us  [run_experts(): lax.all_to_all(outputs, 'dp', split_axis=0, concat_axis=0, tiled=True)]
  transfers between devices with their start and end apart: 7 -> 10, of which waited for: 6 -> 7; matrix products, arithmetic and copies ran while one was open for 4% -> 41% of each run, Pallas kernels for 0% -> 0%
where the time goes in v1:
time: 466 us; the launch traced here: 462 us
  waiting for transfers between devices  205 us (44%)
  local copies, waits for them, and re-layouts  174 us (37%)
  matrix products  32.2 us (7%)
  starting transfers between devices  25.1 us (5%)
  between operations  15.3 us (3%)
  other arithmetic  10.9 us (2%)
    scatter x1, local copies, waits for them, and re-layouts, on_device(): buffer.at[expert_ids, slot_index].set(normed_rows[sources])  138 us
    all_to_all x1, waiting for transfers between devices, on_device(): lax.all_to_all(buffer.at[expert_ids, slot_index].set(normed_rows[sources]...  104 us
    psum x1, waiting for transfers between devices, on_device(): summed_heads = lax.psum(partial_value, 'mp')  50.5 us
    ppermute x2, waiting for transfers between devices, carry_spans_over_axis(): ppermute(n_now, chip_axis, [(b, (b + 1) % met_up) for b in range(met_up)])  27.7 us
    all_to_all x1, waiting for transfers between devices, run_experts(): lax.all_to_all(outputs, 'dp', split_axis=0, concat_axis=0, tiled=True)  12.9 us
    all_to_all x1, starting transfers between devices, on_device(): lax.all_to_all(buffer.at[expert_ids, slot_index].set(normed_rows[sources]...  10.8 us
    all_to_all x1, starting transfers between devices, run_experts(): lax.all_to_all(outputs, 'dp', split_axis=0, concat_axis=0, tiled=True)  10.4 us
  transfers between devices with their start and end apart: 10, of which 7 were waited for; matrix products, arithmetic and copies ran while one was open for 41% of the time, Pallas kernels for 0%

profile of v1, /device:TPU:8, one launch (start us, length us, event | category | flops | bytes accessed | tf_op | source)
XLA Modules:
  0.0 462.5 jit_solution(6194612432282783075)
XLA Ops:
  10.7 21.6 %while.10 = (s32[]{:T(128)}, bf16[2,256,128]{2,1,0:T(8,128)(2,1)S(1)}, s32[2]{0:T(128)}, bf16[2,256,128]{2,1,0:T(8,128)(2,1)S(1)}, s32[2,32]{1,0:T(2,128)}, /*in...) while((s32[]{:T(128)}, ...), condition=%wide.region_5.6_spmd, body=%wide.region_0.5_spmd.sunk | while | flops 554947200 | bytes 23845564 | solution.py:49
  11.4 3.9 gather_fusion
  22.2 3.9 gather_fusion
  37.5 50.5 %all-reduce.2.cloned.1.call-done = f32[128,2048]{1,0:T(8,128)} async-done(((f32[128,2048]{1,0:T(8,128)}), f32[128,2048]{1,0:T(8,128)}) %all-reduce.2.cloned.1.call-update) | async-done | bytes 1048592 | tf_op jit(solution)/shard_map/psum | solution.py:158
  90.4 4.3 gather_fusion.1
  94.7 2.5 broadcast_in_dim.51
  97.2 137.9 %scatter_fusion = bf16[64,16,2048]{2,1,0:T(8,128)(2,1)} fusion(bf16[64,16,2048]{2,1,0:T(8,128)(2,1)} %broadcast_in_dim.51, s32[768]{0:T(1024)S(1)} %get-tuple-element.54, bf16[768,2048]{1,0:T(8,128)(2,1)} %gather_fusion.1), kind=kCustom, calls=%fused_computation.3 | custom fusion | bytes 9443328 | tf_op jit(solution)/shard_map/scatter | solution.py:165
  235.1 10.8 %all-to-all-start = ((bf16[64,16,2048]{2,1,0:T(8,128)(2,1)}), bf16[64,16,2048]{2,1,0:T(8,128)(2,1)}, u32[]{:S(2)}, u32[]{:S(2)}) async-start(bf16[64,16,2048]{2,1,0:T(8,128)(2,1)} %scatter_fusion), calls=%async_computation.1 | async-start | bytes 8388608 | tf_op jit(solution)/shard_map/all_to_all | solution.py:164
  247.1 104.2 %all-to-all-done = bf16[64,16,2048]{2,1,0:T(8,128)(2,1)} async-done(((bf16[64,16,2048]{2,1,0:T(8,128)(2,1)}), bf16[64,16,2048]{2,1,0:T(8,128)(2,1)}, u32[]{:S(2)}, u32[]{:S(2)}) %all-to-all-start) | async-done | bytes 4194336 | tf_op jit(solution)/shard_map/all_to_all | solution.py:164
  351.2 4.3 fusion.35
  357.5 5.2 %constant_dynamic-update-slice_fusion.3 = (bf16[1024,1408]{0,1:T(8,128)(2,1)}, bf16[1024,352]{0,1:T(8,128)(2,1)}) fusion(bf16[1024,1408]{0,1:T(8,128)(2,1)} %broadcast_in_dim.50, s32[]{:T(128)S(6)} %select_n.111, bf16[1024,2048]{1,0:T(8,128)(2,1)} %bitcast.17, bf16[1,2048,352]{1,2,0:T(8,128)(2,1)S(1)} %copy-done.6, f32[1024,352]{0,1:T(8,128)S(1)} %fusion.35), kind=kOutput, calls=%fused_computation.101 | convolution fusion | flops 1478557696 | bytes 8519684 | tf_op jit(solution)/shard_map/dot_general | solution.py:80
  363.4 2.5 collective-permute-start.1
  365.9 14.2 %collective-permute-done = bf16[1024,352]{0,1:T(8,128)(2,1)S(1)} collective-permute-done((bf16[1024,352]{0,1:T(8,128)(2,1)}, bf16[1024,352]{0,1:T(8,128)(2,1)S(1)}, u32[]{:S(2)}, u32[]{:S(2)}) %collective-permute-start) | collective-permute-done | bytes 720928 | tf_op jit(solution)/shard_map/ppermute | solution.py:64
  381.1 2.0 constant_dynamic-update-slice_fusion.1
  383.1 13.5 %collective-permute-done.2 = bf16[1024,352]{0,1:T(8,128)(2,1)} collective-permute-done((bf16[1024,352]{0,1:T(8,128)(2,1)S(1)}, bf16[1024,352]{0,1:T(8,128)(2,1)}, u32[]{:S(2)}, u32[]{:S(2)}) %collective-permute-start.2) | collective-permute-done | bytes 720928 | tf_op jit(solution)/shard_map/ppermute | solution.py:64
  398.6 4.6 convolution_convert_fusion.1
  403.2 10.4 %all-to-all-start.1 = ((bf16[64,16,512]{2,1,0:T(8,128)(2,1)}), bf16[64,16,512]{2,1,0:T(8,128)(2,1)}, u32[]{:S(2)}, u32[]{:S(2)}) async-start(bf16[64,16,512]{2,1,0:T(8,128)(2,1)} %bitcast.139), calls=%async_computation.2 | async-start | bytes 2097152 | tf_op jit(solution)/shard_map/all_to_all | solution.py:87
  413.9 3.2 fusion.67
  417.2 5.1 %all-gather.8.cloned.1.call-done = bf16[704,2048]{0,1:T(8,128)(2,1)} async-done(((bf16[704,32]{0,1:T(8,128)(2,1)}), bf16[704,2048]{0,1:T(8,128)(2,1)}) %all-gather.8.cloned.1.call-update) | async-done | bytes 2883600 | tf_op jit(solution)/shard_map/all_gather | solution.py:104
  422.3 7.0 %convolution_convert_fusion = bf16[128,2048]{1,0:T(8,128)(2,1)} fusion(bf16[704,2048]{0,1:T(8,128)(2,1)} %all-gather.8.cloned.1.call-done, bf16[128,2048]{1,0:T(8,128)(2,1)S(1)} %fusion.43, bf16[2048,704]{1,0:T(8,128)(2,1)} %all-gather.6.cloned.1.call-done, f32[128,704]{0,1:T(8,128)S(1)} %fusion.67), kind=kOutput, calls=%fused_computation.44 | convolution fusion | flops 739000320 | bytes 7176192 | tf_op jit(solution)/shard_map/dot_general | solution.py:102
  429.5 12.9 %all-to-all-done.1 = bf16[64,16,512]{2,1,0:T(8,128)(2,1)} async-done(((bf16[64,16,512]{2,1,0:T(8,128)(2,1)}), bf16[64,16,512]{2,1,0:T(8,128)(2,1)}, u32[]{:S(2)}, u32[]{:S(2)}) %all-to-all-start.1) | async-done | bytes 1048608 | tf_op jit(solution)/shard_map/all_to_all | solution.py:87
  442.4 4.1 gather_fusion.2
  447.7 2.2 fusion.68
  449.9 3.3 reduce-scatter.2.cloned.1.call-done
  (95 shorter events, 34.6 us)
Async XLA Ops:
  7.4 25.1 %copy-start = (bf16[512,2048]{1,0:T(8,128)(2,1)S(1)}, bf16[512,2048]{1,0:T(8,128)(2,1)}, u32[]{:S(2)}) copy-start(bf16[512,2048]{1,0:T(8,128)(2,1)} %param.25) | copy-start | bytes 6291460
  7.4 80.6 %all-reduce.2.cloned.1.call-start = ((), (), s32[]{:S(2)}) async-start(), calls=%async_computation.3 | async-start | bytes 2097152 | tf_op jit(solution)/shard_map/psum | solution.py:158
  15.3 1.7 copy-start.8
  26.1 1.7 copy-start.8
  32.3 2.2 copy-start.4
  32.5 55.5 %copy-start.2 = (bf16[128,2048]{1,0:T(8,128)(2,1)S(1)}, bf16[128,2048]{1,0:T(8,128)(2,1)}, u32[]{:S(2)}) copy-start(bf16[128,2048]{1,0:T(8,128)(2,1)} %param.26) | copy-start | bytes 1572868
  34.0 56.2 %copy-start.3 = (f32[2048]{0:T(1024)S(1)}, f32[2048]{0:T(1024)}, u32[]{:S(2)}) copy-start(f32[2048]{0:T(1024)} %param.27) | copy-start | bytes 24580
  34.0 379.9 %all-gather.4.cloned.1.call-start = ((), (), s32[]{:S(2)}) async-start(), calls=%async_computation.4 | async-start | bytes 3194880 | tf_op jit(solution)/shard_map/all_gather | solution.py:93
  89.4 0.8 copy-start.1
  235.1 116.2 %all-to-all-start = ((bf16[64,16,2048]{2,1,0:T(8,128)(2,1)}), bf16[64,16,2048]{2,1,0:T(8,128)(2,1)}, u32[]{:S(2)}, u32[]{:S(2)}) async-start(bf16[64,16,2048]{2,1,0:T(8,128)(2,1)} %scatter_fusion), calls=%async_computation.1 | async-start | bytes 8388608 | tf_op jit(solution)/shard_map/all_to_all | solution.py:164
  245.9 171.3 %all-gather.6.cloned.1.call-start = ((), (), s32[]{:S(2)}) async-start(), calls=%async_computation.5 | async-start | bytes 3194880 | tf_op jit(solution)/shard_map/all_gather | solution.py:98
  246.5 175.8 %all-gather.8.cloned.1.call-start = ((), (), s32[]{:S(2)}) async-start(), calls=%async_computation.6 | async-start | bytes 3194880 | tf_op jit(solution)/shard_map/all_gather | solution.py:104
  355.5 2.0 copy-start.6
  362.7 17.4 %collective-permute-start = (bf16[1024,352]{0,1:T(8,128)(2,1)}, bf16[1024,352]{0,1:T(8,128)(2,1)S(1)}, u32[]{:S(2)}, u32[]{:S(2)}) collective-permute-start(bf16[1024,352]{0,1:T(8,128)(2,1)} %get-tuple-element.84), channel_id=1, source_target_pairs={{0,1},{1,2},{2,3},{3,0},{4,5},{5,6},{6,7},{7,4},{8,9},{9,10},{10,1... | collective-permute-start | bytes 2162696 | tf_op jit(solution)/shard_map/ppermute | solution.py:64
  363.4 17.7 %collective-permute-start.1 = (bf16[1024,352]{0,1:T(8,128)(2,1)}, bf16[1024,352]{0,1:T(8,128)(2,1)}, u32[]{:S(2)}, u32[]{:S(2)}) collective-permute-start(bf16[1024,352]{0,1:T(8,128)(2,1)} %get-tuple-element.84), channel_id=1, source_target_pairs={{0,3},{1,0},{2,1},{3,2},{4,7},{5,4},{6,5},{7,6},{8,11},{9,8},{10,9... | collective-permute-start | bytes 2162696 | tf_op jit(solution)/shard_map/ppermute | solution.py:69
  380.1 16.4 %collective-permute-start.2 = (bf16[1024,352]{0,1:T(8,128)(2,1)S(1)}, bf16[1024,352]{0,1:T(8,128)(2,1)}, u32[]{:S(2)}, u32[]{:S(2)}) collective-permute-start(bf16[1024,352]{0,1:T(8,128)(2,1)S(1)} %collective-permute-done), channel_id=1, source_target_pairs={{0,1},{1,2},{2,3},{3,0},{4,5},{5,6},{6,7},{7,4},{8,9},{9,10},{10,1... | collective-permute-start | bytes 2162696 | tf_op jit(solution)/shard_map/ppermute | solution.py:64
  380.1 18.4 %copy-start.7 = (bf16[1,1408,512]{2,1,0:T(8,128)(2,1)S(1)}, bf16[1,1408,512]{2,1,0:T(8,128)(2,1)}, u32[]{:S(2)}) copy-start(bf16[1,1408,512]{2,1,0:T(8,128)(2,1)} %param.32) | copy-start | bytes 4325380
  403.2 39.2 %all-to-all-start.1 = ((bf16[64,16,512]{2,1,0:T(8,128)(2,1)}), bf16[64,16,512]{2,1,0:T(8,128)(2,1)}, u32[]{:S(2)}, u32[]{:S(2)}) async-start(bf16[64,16,512]{2,1,0:T(8,128)(2,1)} %bitcast.139), calls=%async_computation.2 | async-start | bytes 2097152 | tf_op jit(solution)/shard_map/all_to_all | solution.py:87
  413.6 39.6 %reduce-scatter.2.cloned.1.call-start = ((), (), s32[]{:S(2)}) async-start(), calls=%async_computation.7 | async-start | bytes 655360 | tf_op jit(solution)/shard_map/reduce_scatter | solution.py:107
  417.1 12.2 %copy-start.5 = (f32[128,6]{0,1:T(8,128)S(1)}, f32[128,6]{0,1:T(8,128)}, u32[]{:S(2)}) copy-start(f32[128,6]{0,1:T(8,128)} %param.29) | copy-start | bytes 9220
Sparse Core Ops, SparseCore 0:
  34.1 53.7 all-reduce.1
  429.5 23.7 reduce-scatter.1
Sparse Core Ops, SparseCore 1:
  37.6 80.1 all-gather.3
  249.5 92.7 all-gather.5
  345.2 77.0 all-gather.7
